TPU v7x, 512 devices: a whole 4x8x8 slice. The times are simulated.
512 devices in a mesh: wide: 64 (over z, x, core), narrow: 8 (over y).
Axes of the slice: x: 4, y: 8, z: 8, core: 2. Of those that a mesh axis runs over, the one named last changes fastest.
Arguments:
- hidden_in: bfloat16 [16384, 2048], P('wide', 'narrow'), may hold values from -6 to 6
- segment_ids: int32 [16384], P('wide'), may hold values from 0 to 31, never falling along the last dimension, each value on 1 to 2048 neighbouring positions
- page_table: int32 [1024], P('wide'), may hold values from 0 to 1023, as said below
- wq: bfloat16 [2048, 2048], P('wide', 'narrow')
- wk: bfloat16 [2048, 2048], P('wide', 'narrow')
- wv: bfloat16 [2048, 2048], P('wide', 'narrow'), may hold values from -0.125 to 0.125
- wo: bfloat16 [2048, 2048], P('narrow', 'wide'), may hold values from -0.125 to 0.125
- wg: bfloat16 [2048, 4096], P('wide', 'narrow'), may hold values from -0.125 to 0.125
- wu: bfloat16 [2048, 4096], P('wide', 'narrow'), may hold values from -0.125 to 0.125
- wd: bfloat16 [4096, 2048], P('narrow', 'wide'), may hold values from -0.09375 to 0.09375
Outputs:
- result: bfloat16 [16384, 2048], P('wide', 'narrow')
- kv_cache: bfloat16 [2, 1024, 16, 2048], P(None, 'wide', None, 'narrow')
Inputs may be any that keep to these rules, and one draw needn't show every extreme that they name: `page_table`: entries 16 * w to 16 * (w + 1) - 1 of the table are a permutation of those same numbers, for every w.
All inputs are finite; a program needn't handle non-finite values.
Results may differ from a plain program's by a relative error of at most 0.017.
Values may be sent and summed in bfloat16 or wider, within the bound.
No kernel may reach another device: no remote copies, remote signals or barrier semaphores. Data moves between devices by JAX's collectives and lax.ppermute only.
A program may use at most 64 MiB of HBM per device.

v0:
```python
import jax
import jax.numpy as jnp
from jax import lax
from jax.sharding import PartitionSpec as P

HEAD_DIM = 128
REACH = 8
PAGE = 16
epsilon = 1e-05
rope_base = 10000.0


def prefix(value, axis, join, neutral):
    count, mine = (lax.axis_size(axis), lax.axis_index(axis))
    pieces = jax.tree.map(lambda part: lax.all_gather(part, axis), value)
    running = jax.tree.map(
        lambda part, zero: jnp.full_like(part, 0) + jnp.asarray(zero, part.dtype), value, neutral
    )

    def lap(position, running):
        longer = join(running, jax.tree.map(lambda part: part[position], pieces))
        return jax.tree.map(lambda new, old: jnp.where(position < mine, new, old), longer, running)

    return lax.fori_loop(0, count - 1, lap, running)


def shifted(value, axis, steps):
    count = lax.axis_size(axis)
    first, last = (max(0, -steps), min(count, count - steps))
    return lax.ppermute(value, axis, [(source, source + steps) for source in range(first, last)])


def norm_rows(source):
    widened = source.astype(jnp.float32)
    center = widened - jnp.mean(widened, axis=-1, keepdims=True)
    spread = jnp.mean(center * center, axis=-1, keepdims=True)
    return (center * lax.rsqrt(spread + epsilon)).astype(jnp.bfloat16)


def rotate(projected, positions):
    head_size = projected.shape[-1]
    half_dim = head_size // 2
    frequency = jnp.power(rope_base, -jnp.arange(half_dim, dtype=jnp.float32) * 2.0 / head_size)
    angles = positions.astype(jnp.float32)[:, None] * frequency[None, :]
    cosine = jnp.cos(angles)[:, None, :]
    sine_part = jnp.sin(angles)[:, None, :]
    first_half = projected[..., :half_dim]
    second_half = projected[..., half_dim:]
    return jnp.concatenate(
        [
            first_half * cosine - second_half * sine_part,
            second_half * cosine + first_half * sine_part,
        ],
        axis=-1,
    )


def join_runs(earlier, later):
    early_last, early_trailing, early_single = earlier
    late_last, late_trailing, late_single = later
    late_empty = late_trailing == 0
    same_id = (early_last == late_last).astype(jnp.int32)
    linked = (late_single == 1) & (same_id == 1) & (early_trailing > 0)
    last_id = jnp.where(late_empty, early_last, late_last)
    trailing = jnp.where(
        late_empty, early_trailing, late_trailing + jnp.where(linked, early_trailing, 0)
    )
    single = jnp.where(
        late_empty,
        early_single,
        jnp.where(early_trailing == 0, late_single, late_single * early_single * same_id),
    )
    return (last_id, trailing, single)


def add_rows(source, piece):
    return jnp.dot(source, piece, preferred_element_type=jnp.float32)


def per_device(hidden_in, segment_ids, page_table, wq, wk, wv, wo, wg, wu, wd):
    tok_rows = hidden_in.shape[0]
    wide_rank = lax.axis_index("wide")
    local_index = jnp.arange(tok_rows, dtype=jnp.int32)
    run_last = segment_ids[tok_rows - 1]
    run_trailing = jnp.sum((segment_ids == run_last).astype(jnp.int32))
    run_single = (segment_ids[0] == run_last).astype(jnp.int32)
    earlier = prefix(
        (run_last, run_trailing, run_single),
        "wide",
        join_runs,
        (jnp.int32(-1), jnp.int32(0), jnp.int32(1)),
    )
    lower_count = jnp.sum((segment_ids[None, :] < segment_ids[:, None]).astype(jnp.int32), axis=1)
    carried = jnp.where(
        (segment_ids == earlier[0]) & (segment_ids == segment_ids[0]), earlier[1], 0
    )
    positions = local_index - lower_count + carried
    global_index = wide_rank * tok_rows + local_index
    query_start = global_index - positions
    whole = lax.all_gather(hidden_in, "narrow", axis=1, tiled=True)
    normed = norm_rows(whole)
    local_width = wq.shape[1]
    head_count = local_width // HEAD_DIM

    def add_normed(piece):
        return add_rows(normed, piece)

    q_proj = add_normed(lax.all_gather(wq, "wide", axis=0, tiled=True))
    k_proj = add_normed(lax.all_gather(wk, "wide", axis=0, tiled=True))
    v_proj = add_normed(lax.all_gather(wv, "wide", axis=0, tiled=True))
    queries = rotate(q_proj.reshape(tok_rows, head_count, HEAD_DIM), positions).astype(jnp.bfloat16)
    keys_rot = rotate(k_proj.reshape(tok_rows, head_count, HEAD_DIM), positions).astype(
        jnp.bfloat16
    )
    values = v_proj.astype(jnp.bfloat16).reshape(tok_rows, head_count, HEAD_DIM)
    current = (keys_rot, values)
    blocks = [current]
    for step_back in range(REACH):
        current = shifted((current[0], current[1]), "wide", 1)
        blocks.append(current)
    score_scale = HEAD_DIM ** (-0.5)
    ordered = blocks[::-1]
    key_all = jnp.concatenate([member[0] for member in ordered], axis=0)
    value_all = jnp.concatenate([member[1] for member in ordered], axis=0)
    key_index = (wide_rank - REACH) * tok_rows + jnp.arange((REACH + 1) * tok_rows, dtype=jnp.int32)
    allowed = (key_index[None, :] >= query_start[:, None]) & (
        key_index[None, :] <= global_index[:, None]
    )
    scores = (
        jnp.einsum("qhd,khd->hqk", queries, key_all, preferred_element_type=jnp.float32)
        * score_scale
    )
    scores = jnp.where(allowed[None], scores, -1e30)
    row_peak = jnp.max(scores, axis=-1, keepdims=True)
    exps = jnp.where(allowed[None], jnp.exp(scores - row_peak), 0.0)
    attn_probs = (exps / jnp.sum(exps, axis=-1, keepdims=True)).astype(jnp.bfloat16)
    mixed = jnp.einsum("hqk,khd->qhd", attn_probs, value_all, preferred_element_type=jnp.float32)
    attended = mixed.astype(jnp.bfloat16).reshape(tok_rows, local_width)
    attn_terms = jnp.dot(
        attended, lax.all_gather(wo, "wide", axis=1, tiled=True), preferred_element_type=jnp.float32
    )
    attn_sum = lax.psum_scatter(
        attn_terms.astype(jnp.bfloat16), "narrow", scatter_dimension=1, tiled=True
    ).astype(jnp.float32)
    first_res = (hidden_in.astype(jnp.float32) + attn_sum).astype(jnp.bfloat16)
    whole_two = lax.all_gather(first_res, "narrow", axis=1, tiled=True)
    normed_two = norm_rows(whole_two)

    def add_second(piece):
        return add_rows(normed_two, piece)

    gate_proj = add_second(lax.all_gather(wg, "wide", axis=0, tiled=True))
    up_proj = add_second(lax.all_gather(wu, "wide", axis=0, tiled=True))
    hidden = (jax.nn.silu(gate_proj) * up_proj).astype(jnp.bfloat16)
    down_terms = jnp.dot(
        hidden, lax.all_gather(wd, "wide", axis=1, tiled=True), preferred_element_type=jnp.float32
    )
    down_sum = lax.psum_scatter(
        down_terms.astype(jnp.bfloat16), "narrow", scatter_dimension=1, tiled=True
    ).astype(jnp.float32)
    result = (first_res.astype(jnp.float32) + down_sum).astype(jnp.bfloat16)
    page_count = tok_rows // PAGE
    slots = page_table - wide_rank * page_count
    pairs = jnp.stack(
        [
            keys_rot.reshape(page_count, PAGE, local_width),
            values.reshape(page_count, PAGE, local_width),
        ],
        axis=0,
    )
    kv_cache = jnp.zeros_like(pairs).at[:, slots].set(pairs)
    return (result, kv_cache)


def solution(mesh):
    return jax.shard_map(
        per_device,
        mesh=mesh,
        in_specs=(
            P("wide", "narrow"),
            P("wide"),
            P("wide"),
            P("wide", "narrow"),
            P("wide", "narrow"),
            P("wide", "narrow"),
            P("narrow", "wide"),
            P("wide", "narrow"),
            P("wide", "narrow"),
            P("narrow", "wide"),
        ),
        out_specs=(P("wide", "narrow"), P(None, "wide", None, "narrow")),
        check_vma=False,
    )
```

profile of v0, /device:TPU:2, one launch (start us, length us, event | category | flops | bytes accessed | tf_op | source)
XLA Modules:
  0.0 878.4 jit_solution(14633172779645840433)
XLA Ops:
  11.0 1.3 dynamic-slice
  12.3 2.0 fusion.47
  14.3 2.0 fusion.27
  18.3 1.4 dynamic-update-slice
  19.8 25.7 %all-reduce.3 = (s32[64]{0:T(128)S(1)}, s32[64]{0:T(128)S(1)}, s32[64]{0:T(128)S(1)}) all-reduce(s32[64]{0:T(128)S(1)} %dynamic-update-slice, s32[64]{0:T(128)S(1)} %get-tuple-element.159, s32[64]{0:T(128)S(1)} %dynamic-update-slice.2), channel_id=1, replica_groups=mesh['wide'=64,'narrow'=8] {'wide'}, use_global_device_ids=true, to_apply=%add | all-reduce | flops 192 | bytes 1536
  45.5 335.9 %while.15 = (s32[]{:T(128)}, s32[]{:T(128)}, s32[]{:T(128)}, s32[]{:T(128)}, s32[64]{0:T(128)S(1)}, /*index=5*/s32[64]{0:T(128)S(1)}, s32[64]{0:T(128)S(1)}, s32[]{:T(128)}, s32[]{:T(128)}, s32[1]{0:T(128)}) while((s32[]{:T(128)}, s32[]{:T(128)}, s32[]{:T(128)}, s32[]{:T(128)}, s32[64]{0:T(128)S(1)}, /*index=5*/s32[64]{0:T(128)S(1)}, ...), condition=%wide.region_5.6_spmd, body=%wide.region_4.5_spmd.sunk | while | flops 17 | bytes 279 | solution.py:24
  381.3 1.3 fusion.43
  383.2 1.5 convert_reduce_fusion.1
  385.6 1.7 fusion.52
  387.8 1.9 collective-permute-start.8
  389.8 1.7 convolution_convert_fusion.2
  391.6 2.5 collective-permute-start
  394.1 1.9 collective-permute-start.9
  396.1 1.8 collective-permute-done
  397.9 1.9 collective-permute-start.1
  400.4 1.9 collective-permute-start.10
  402.4 1.7 collective-permute-done.1
  404.1 1.9 collective-permute-start.2
  406.7 1.9 collective-permute-start.11
  408.6 1.8 collective-permute-done.2
  410.4 2.2 collective-permute-start.3
  413.1 3.3 collective-permute-start.12
  416.9 4.6 collective-permute-start.4
  421.6 3.6 collective-permute-start.13
  425.2 1.7 fusion.51
  427.0 4.6 collective-permute-start.5
  431.7 3.7 collective-permute-start.14
  435.7 4.7 collective-permute-start.6
  440.4 3.2 collective-permute-start.15
  444.4 5.0 collective-permute-start.7
  452.5 1.4 constant_dynamic-update-slice_fusion.5
  454.0 1.0 copy-done.8
  455.0 5.9 fusion.48
  460.9 3.7 fusion.15
  464.6 22.8 %all-gather.18.cloned.1.call-done = bf16[256,2048]{0,1:T(8,128)(2,1)} async-done(((bf16[256,32]{0,1:T(8,128)(2,1)}), bf16[256,2048]{0,1:T(8,128)(2,1)}) %all-gather.18.cloned.1.call-update) | async-done | bytes 1048592 | tf_op jit(solution)/shard_map/all_gather | solution.py:140
  487.4 2.7 convolution_convert_fusion.1
  490.2 39.1 %reduce-scatter.3.cloned.1.call-done = bf16[256,256]{1,0:T(8,128)(2,1)} async-done(((bf16[256,2048]{1,0:T(8,128)(2,1)}), bf16[256,256]{1,0:T(8,128)(2,1)}) %reduce-scatter.3.cloned.1.call-update) | async-done | bytes 131088 | tf_op jit(solution)/shard_map/reduce_scatter | solution.py:142
  529.3 1.6 add_convert_fusion.1
  533.2 40.0 %all-gather.20.cloned.1.call-done = bf16[256,2048]{1,0:T(8,128)(2,1)} async-done(((bf16[256,256]{1,0:T(8,128)(2,1)}), bf16[256,2048]{1,0:T(8,128)(2,1)}) %all-gather.20.cloned.1.call-update) | async-done | bytes 1048592 | tf_op jit(solution)/shard_map/all_gather | solution.py:146
  573.2 1.5 convert_reduce_fusion
  575.2 83.4 %all-gather.22.cloned.1.call-done = bf16[2048,512]{1,0:T(8,128)(2,1)} async-done(((bf16[32,512]{1,0:T(8,128)(2,1)}), bf16[2048,512]{1,0:T(8,128)(2,1)}) %all-gather.22.cloned.1.call-update) | async-done | bytes 2097168 | tf_op jit(solution)/shard_map/all_gather | solution.py:152
  658.6 2.3 fusion.41
  660.9 81.6 %all-gather.24.cloned.1.call-done = bf16[2048,512]{1,0:T(8,128)(2,1)} async-done(((bf16[32,512]{1,0:T(8,128)(2,1)}), bf16[2048,512]{1,0:T(8,128)(2,1)}) %all-gather.24.cloned.1.call-update) | async-done | bytes 2097168 | tf_op jit(solution)/shard_map/all_gather | solution.py:153
  742.6 83.8 %all-gather.26.cloned.1.call-done = bf16[512,2048]{0,1:T(8,128)(2,1)} async-done(((bf16[512,32]{0,1:T(8,128)(2,1)}), bf16[512,2048]{0,1:T(8,128)(2,1)}) %all-gather.26.cloned.1.call-update) | async-done | bytes 2097168 | tf_op jit(solution)/shard_map/all_gather | solution.py:156
  826.4 4.7 convolution_convert_fusion
  831.5 1.2 scatter_fusion
  832.7 37.6 %reduce-scatter.5.cloned.1.call-done = bf16[256,256]{1,0:T(8,128)(2,1)} async-done(((bf16[256,2048]{1,0:T(8,128)(2,1)}), bf16[256,256]{1,0:T(8,128)(2,1)}) %reduce-scatter.5.cloned.1.call-update) | async-done | bytes 131088 | tf_op jit(solution)/shard_map/reduce_scatter | solution.py:158
  870.3 1.6 add_convert_fusion
  (297 shorter events, 139.8 us)
Async XLA Ops:
  7.2 376.1 %all-gather.10.cloned.1.call-start = ((), (), s32[]{:S(2)}) async-start(), calls=%async_computation.2 | async-start | bytes 1179648 | tf_op jit(solution)/shard_map/all_gather | solution.py:100
  7.9 377.7 %all-gather.16.cloned.1.call-start = ((), (), s32[]{:S(2)}) async-start(), calls=%async_computation.5 | async-start | bytes 1064960 | tf_op jit(solution)/shard_map/all_gather | solution.py:109
  8.6 381.1 %all-gather.12.cloned.1.call-start = ((), (), s32[]{:S(2)}) async-start(), calls=%async_computation.3 | async-start | bytes 1064960 | tf_op jit(solution)/shard_map/all_gather | solution.py:110
  9.4 415.9 %all-gather.14.cloned.1.call-start = ((), (), s32[]{:S(2)}) async-start(), calls=%async_computation.4 | async-start | bytes 1064960 | tf_op jit(solution)/shard_map/all_gather | solution.py:108
  10.0 477.4 %all-gather.18.cloned.1.call-start = ((), (), s32[]{:S(2)}) async-start(), calls=%async_computation.6 | async-start | bytes 1064960 | tf_op jit(solution)/shard_map/all_gather | solution.py:140
  383.2 1.6 copy-start
  387.8 6.3 collective-permute-start.8
  391.6 6.3 collective-permute-start
  394.1 6.3 collective-permute-start.9
  397.9 6.3 collective-permute-start.1
  400.4 6.3 collective-permute-start.10
  402.4 126.9 %reduce-scatter.3.cloned.1.call-start = ((), (), s32[]{:S(2)}) async-start(), calls=%async_computation.7 | async-start | bytes 1179648 | tf_op jit(solution)/shard_map/reduce_scatter | solution.py:142
  404.1 6.3 collective-permute-start.2
  406.7 6.4 collective-permute-start.11
  410.4 6.5 collective-permute-start.3
  413.1 8.5 collective-permute-start.12
  416.9 10.1 %collective-permute-start.4 = (bf16[256,2,128]{0,2,1:T(8,128)(2,1)S(1)}, bf16[256,2,128]{0,2,1:T(8,128)(2,1)}, u32[]{:S(2)}, u32[]{:S(2)}) collective-permute-start(bf16[256,2,128]{0,2,1:T(8,128)(2,1)S(1)} %collective-permute-done.3), channel_id=1, source_target_pairs={{0,8},{8,16},{16,24},{24,32},{32,40},{40,48},{48,56},{56,64},{64,7... | collective-permute-start | bytes 393224 | tf_op jit(solution)/shard_map/ppermute | solution.py:30
  421.6 10.1 %collective-permute-start.13 = (bf16[256,2,128]{2,0,1:T(8,128)(2,1)}, bf16[256,2,128]{2,0,1:T(8,128)(2,1)}, u32[]{:S(2)}, u32[]{:S(2)}) collective-permute-start(bf16[256,2,128]{2,0,1:T(8,128)(2,1)} %collective-permute-done.12), channel_id=1, source_target_pairs={{0,8},{8,16},{16,24},{24,32},{32,40},{40,48},{48,56},{56,64},{64,7... | collective-permute-start | bytes 393224 | tf_op jit(solution)/shard_map/ppermute | solution.py:30
  427.0 8.6 collective-permute-start.5
  431.7 8.7 collective-permute-start.14
  435.7 8.7 collective-permute-start.6
  440.4 8.9 %collective-permute-start.15 = (bf16[256,2,128]{2,0,1:T(8,128)(2,1)S(1)}, bf16[256,2,128]{2,0,1:T(8,128)(2,1)S(1)}, u32[]{:S(2)}, u32[]{:S(2)}) collective-permute-start(bf16[256,2,128]{2,0,1:T(8,128)(2,1)S(1)} %collective-permute-done.14), channel_id=1, source_target_pairs={{0,8},{8,16},{16,24},{24,32},{32,40},{40,48},{48,56},{56,64},{64,7... | collective-permute-start | bytes 393224 | tf_op jit(solution)/shard_map/ppermute | solution.py:30
  444.4 8.1 collective-permute-start.7
  452.4 1.6 copy-start.7
  452.4 2.6 copy-start.5
  452.4 2.6 copy-start.6
  454.0 1.0 copy-start.8
  487.4 41.9 %copy-start.4 = (bf16[256,256]{1,0:T(8,128)(2,1)S(1)}, bf16[256,256]{1,0:T(8,128)(2,1)}, u32[]{:S(2)}) copy-start(bf16[256,256]{1,0:T(8,128)(2,1)} %param.12) | copy-start | bytes 393220
  490.1 83.1 %all-gather.20.cloned.1.call-start = ((), (), s32[]{:S(2)}) async-start(), calls=%async_computation.8 | async-start | bytes 1179648 | tf_op jit(solution)/shard_map/all_gather | solution.py:146
  530.9 127.7 %all-gather.22.cloned.1.call-start = ((), (), s32[]{:S(2)}) async-start(), calls=%async_computation.9 | async-start | bytes 2129920 | tf_op jit(solution)/shard_map/all_gather | solution.py:152
  531.7 210.9 %all-gather.24.cloned.1.call-start = ((), (), s32[]{:S(2)}) async-start(), calls=%async_computation.10 | async-start | bytes 2129920 | tf_op jit(solution)/shard_map/all_gather | solution.py:153
  532.4 294.0 %all-gather.26.cloned.1.call-start = ((), (), s32[]{:S(2)}) async-start(), calls=%async_computation.11 | async-start | bytes 2129920 | tf_op jit(solution)/shard_map/all_gather | solution.py:156
  533.0 337.3 %reduce-scatter.5.cloned.1.call-start = ((), (), s32[]{:S(2)}) async-start(), calls=%async_computation.12 | async-start | bytes 1179648 | tf_op jit(solution)/shard_map/reduce_scatter | solution.py:158
  573.2 1.5 copy-start.1
  660.9 170.2 %copy-start.9 = (s32[16]{0:T(128)S(1)}, s32[16]{0:T(128)}, u32[]{:S(2)}) copy-start(s32[16]{0:T(128)} %param.14) | copy-start | bytes 196
  831.3 39.0 %copy-start.2 = (bf16[256,256]{1,0:T(8,128)(2,1)S(1)}, bf16[256,256]{1,0:T(8,128)(2,1)}, u32[]{:S(2)}) copy-start(bf16[256,256]{1,0:T(8,128)(2,1)} %add_convert_fusion.1) | copy-start | bytes 393220
  832.7 39.2 %copy-start.3 = (bf16[2,16,16,256]{3,2,1,0:T(8,128)(2,1)}, bf16[2,16,16,256]{3,2,1,0:T(8,128)(2,1)S(1)}, u32[]{:S(2)}) copy-start(bf16[2,16,16,256]{3,2,1,0:T(8,128)(2,1)S(1)} %scatter_fusion) | copy-start | bytes 786436
Sparse Core Ops, SparseCore 0:
  10.0 46.6 all-gather.9
  60.1 81.1 all-gather.15
  144.6 79.8 all-gather.11
  227.7 79.7 all-gather.13
  402.5 84.8 all-gather.17
  490.2 38.9 reduce-scatter.2
  531.9 41.2 all-gather.19
  576.6 81.9 all-gather.21
  661.9 80.5 all-gather.23
  745.8 80.5 all-gather.25
  831.2 39.0 reduce-scatter.4
where the time goes:
time: 882 us; the launch traced here: 878 us
  waiting for transfers between devices  400 us (45%)
  loops' own time  212 us (24%)
  local copies, waits for them, and re-layouts  137 us (16%)
  starting transfers between devices  49.6 us (6%)
  blocking collectives  25.7 us (3%)
  matrix products  24.5 us (3%)
  between operations  15.8 us (2%)
  other arithmetic  13.9 us (2%)
    another operation x1, loops' own time, prefix(): return lax.fori_loop(0, count - 1, lap, running)  212 us
    dynamic_slice x189, local copies, waits for them, and re-layouts, lap(): longer = join(running, jax.tree.map(lambda part: part[position], pieces))  124 us
    all_gather x1, waiting for transfers between devices, per_device(): lax.all_gather(wd, 'wide', axis=1, tiled=True)  83.8 us
    all_gather x1, waiting for transfers between devices, per_device(): gate_proj = add_second(lax.all_gather(wg, 'wide', axis=0, tiled=True))  83.4 us
    all_gather x1, waiting for transfers between devices, per_device(): up_proj = add_second(lax.all_gather(wu, 'wide', axis=0, tiled=True))  81.6 us
    ppermute x16, starting transfers between devices, shifted(): lax.ppermute(value, axis, [(source, source + steps) for source in range(f...  49 us
    all_gather x1, waiting for transfers between devices, per_device(): whole_two = lax.all_gather(first_res, 'narrow', axis=1, tiled=True)  40 us
    reduce_scatter x1, waiting for transfers between devices, per_device(): lax.psum_scatter(attn_terms.astype(jnp.bfloat16), 'narrow', scatter_dimen...  39.1 us
  transfers between devices with their start and end apart: 27, of which 13 were waited for; matrix products, arithmetic and copies ran while one was open for 19% of the time, Pallas kernels for 0%

commit v1 on v0

--- a/solution.py
+++ b/solution.py
@@ -2,6 +2,7 @@
 import jax.numpy as jnp
 from jax import lax
 from jax.sharding import PartitionSpec as P
+from jax.lax import all_to_all, axis_size
 
 HEAD_DIM = 128
 REACH = 8
@@ -143,7 +144,15 @@
         attn_terms.astype(jnp.bfloat16), "narrow", scatter_dimension=1, tiled=True
     ).astype(jnp.float32)
     first_res = (hidden_in.astype(jnp.float32) + attn_sum).astype(jnp.bfloat16)
-    whole_two = lax.all_gather(first_res, "narrow", axis=1, tiled=True)
+
+    def _view_row(local_x, mesh_name):
+        reached = jnp.concatenate(
+            all_to_all(jnp.stack([local_x for _ in range(axis_size(mesh_name))]), mesh_name, 0, 0),
+            1,
+        )
+        return reached
+
+    whole_two = _view_row(first_res, "narrow")
     normed_two = norm_rows(whole_two)
 
     def add_second(piece):

time: 882 us -> 813 us (0.922)
  waiting for transfers between devices: 400 us -> 329 us
  blocking collectives: 25.7 us -> 54.6 us
  loops' own time: 212 us -> 193 us
    all_gather x1 -> x0, waiting for transfers between devices: 40 us -> none  [per_device(): whole_two = lax.all_gather(first_res, 'narrow', axis=1, tiled=True)]
    all_gather x1, waiting for transfers between devices: 83.4 us -> 54.2 us  [per_device(): gate_proj = add_second(lax.all_gather(wg, 'wide', axis=0, tiled=True))]
    all_to_all x0 -> x1, blocking collectives: none -> 28.9 us  [_view_row(): all_to_all(jnp.stack([local_x for _ in range(axis_size(mesh_name))]), mes...]
    another operation x1, loops' own time: 212 us -> 193 us  [prefix(): return lax.fori_loop(0, count - 1, lap, running)]
  transfers between devices with their start and end apart: 27 -> 26, of which waited for: 13 -> 12; matrix products, arithmetic and copies ran while one was open for 19% -> 19% of each run, Pallas kernels for 0% -> 0%
where the time goes in v1:
time: 813 us; the launch traced here: 809 us
  waiting for transfers between devices  329 us (40%)
  loops' own time  193 us (24%)
  local copies, waits for them, and re-layouts  130 us (16%)
  blocking collectives  54.6 us (7%)
  starting transfers between devices  49.3 us (6%)
  matrix products  24.2 us (3%)
  between operations  16.1 us (2%)
  other arithmetic  12.1 us (1%)
    another operation x1, loops' own time, prefix(): return lax.fori_loop(0, count - 1, lap, running)  193 us
    dynamic_slice x189, local copies, waits for them, and re-layouts, lap(): longer = join(running, jax.tree.map(lambda part: part[position], pieces))  117 us
    all_gather x1, waiting for transfers between devices, per_device(): lax.all_gather(wd, 'wide', axis=1, tiled=True)  84 us
    all_gather x1, waiting for transfers between devices, per_device(): up_proj = add_second(lax.all_gather(wu, 'wide', axis=0, tiled=True))  81.6 us
    all_gather x1, waiting for transfers between devices, per_device(): gate_proj = add_second(lax.all_gather(wg, 'wide', axis=0, tiled=True))  54.2 us
    ppermute x16, starting transfers between devices, shifted(): lax.ppermute(value, axis, [(source, source + steps) for source in range(f...  48.9 us
    reduce_scatter x1, waiting for transfers between devices, per_device(): lax.psum_scatter(down_terms.astype(jnp.bfloat16), 'narrow', scatter_dimen...  37.7 us
    reduce_scatter x1, waiting for transfers between devices, per_device(): lax.psum_scatter(attn_terms.astype(jnp.bfloat16), 'narrow', scatter_dimen...  37 us
  transfers between devices with their start and end apart: 26, of which 12 were waited for; matrix products, arithmetic and copies ran while one was open for 19% of the time, Pallas kernels for 0%

profile of v1, /device:TPU:2, one launch (start us, length us, event | category | flops | bytes accessed | tf_op | source)
XLA Modules:
  0.0 809.4 jit_solution(17367300782184038188)
XLA Ops:
  10.0 0.9 convert_reduce_fusion.2
  11.0 1.3 dynamic-slice
  12.2 1.9 fusion.41
  14.1 2.0 fusion.25
  18.0 1.3 dynamic-update-slice
  19.3 25.7 %all-reduce.3 = (s32[64]{0:T(128)S(1)}, s32[64]{0:T(128)S(1)}, s32[64]{0:T(128)S(1)}) all-reduce(s32[64]{0:T(128)S(1)} %dynamic-update-slice, s32[64]{0:T(128)S(1)} %get-tuple-element.159, s32[64]{0:T(128)S(1)} %dynamic-update-slice.2), channel_id=1, replica_groups=mesh['wide'=64,'narrow'=8] {'wide'}, use_global_device_ids=true, to_apply=%add | all-reduce | flops 192 | bytes 1536
  45.0 310.9 %while.15 = (s32[]{:T(128)}, s32[]{:T(128)}, s32[]{:T(128)}, s32[]{:T(128)}, s32[64]{0:T(128)S(1)}, /*index=5*/s32[64]{0:T(128)S(1)}, s32[64]{0:T(128)S(1)}, s32[]{:T(128)}, s32[]{:T(128)}, s32[1]{0:T(128)}) while((s32[]{:T(128)}, s32[]{:T(128)}, s32[]{:T(128)}, s32[]{:T(128)}, s32[64]{0:T(128)S(1)}, /*index=5*/s32[64]{0:T(128)S(1)}, ...), condition=%wide.region_5.6_spmd, body=%wide.region_4.5_spmd.sunk | while | flops 17 | bytes 279 | solution.py:25
  356.0 1.2 fusion.37
  357.8 1.5 convert_reduce_fusion
  360.2 1.7 fusion.46
  362.4 1.9 collective-permute-start.8
  364.4 1.7 convolution_convert_fusion.2
  366.1 2.5 collective-permute-start
  368.7 1.9 collective-permute-start.9
  370.6 1.8 collective-permute-done
  372.4 1.9 collective-permute-start.1
  375.0 1.9 collective-permute-start.10
  377.0 1.7 collective-permute-done.1
  378.7 1.9 collective-permute-start.2
  381.2 1.9 collective-permute-start.11
  383.2 1.8 collective-permute-done.2
  385.0 2.2 collective-permute-start.3
  387.6 3.3 collective-permute-start.12
  391.5 4.6 collective-permute-start.4
  396.1 3.6 collective-permute-start.13
  399.8 1.7 fusion.45
  401.6 4.6 collective-permute-start.5
  406.2 3.7 collective-permute-start.14
  410.2 4.7 collective-permute-start.6
  415.0 3.1 collective-permute-start.15
  418.9 5.0 collective-permute-start.7
  427.1 1.4 constant_dynamic-update-slice_fusion.5
  428.6 1.0 copy-done.6
  429.6 6.0 fusion.42
  435.6 3.3 fusion.13
  438.9 23.0 %all-gather.17.cloned.1.call-done = bf16[256,2048]{0,1:T(8,128)(2,1)} async-done(((bf16[256,32]{0,1:T(8,128)(2,1)}), bf16[256,2048]{0,1:T(8,128)(2,1)}) %all-gather.17.cloned.1.call-update) | async-done | bytes 1048592 | tf_op jit(solution)/shard_map/all_gather | solution.py:141
  461.9 2.8 convolution_convert_fusion.1
  467.0 37.0 %reduce-scatter.3.cloned.1.call-done = bf16[256,256]{1,0:T(8,128)(2,1)} async-done(((bf16[256,2048]{1,0:T(8,128)(2,1)}), bf16[256,256]{1,0:T(8,128)(2,1)}) %reduce-scatter.3.cloned.1.call-update) | async-done | bytes 131088 | tf_op jit(solution)/shard_map/reduce_scatter | solution.py:143
  504.0 0.9 add_convert_fusion.1
  505.1 28.9 %all_to_all.5 = bf16[8,256,256]{1,2,0:T(8,128)(2,1)S(1)} all-to-all(bf16[8,256,256]{1,2,0:T(8,128)(2,1)S(1)} %stack.4), channel_id=1, replica_groups=mesh['wide'=64,'narrow'=8] {'narrow'}, dimensions={0} | all-to-all | bytes 2097152 | tf_op jit(solution)/shard_map/all_to_all | solution.py:150
  534.9 54.2 %all-gather.19.cloned.1.call-done = bf16[2048,512]{1,0:T(8,128)(2,1)} async-done(((bf16[32,512]{1,0:T(8,128)(2,1)}), bf16[2048,512]{1,0:T(8,128)(2,1)}) %all-gather.19.cloned.1.call-update) | async-done | bytes 2097168 | tf_op jit(solution)/shard_map/all_gather | solution.py:161
  589.1 2.3 fusion.47
  591.4 81.6 %all-gather.21.cloned.1.call-done = bf16[2048,512]{1,0:T(8,128)(2,1)} async-done(((bf16[32,512]{1,0:T(8,128)(2,1)}), bf16[2048,512]{1,0:T(8,128)(2,1)}) %all-gather.21.cloned.1.call-update) | async-done | bytes 2097168 | tf_op jit(solution)/shard_map/all_gather | solution.py:162
  673.1 84.0 %all-gather.23.cloned.1.call-done = bf16[512,2048]{0,1:T(8,128)(2,1)} async-done(((bf16[512,32]{0,1:T(8,128)(2,1)}), bf16[512,2048]{0,1:T(8,128)(2,1)}) %all-gather.23.cloned.1.call-update) | async-done | bytes 2097168 | tf_op jit(solution)/shard_map/all_gather | solution.py:165
  757.1 4.6 convolution_convert_fusion
  762.1 1.2 scatter_fusion
  763.3 37.7 %reduce-scatter.5.cloned.1.call-done = bf16[256,256]{1,0:T(8,128)(2,1)} async-done(((bf16[256,2048]{1,0:T(8,128)(2,1)}), bf16[256,256]{1,0:T(8,128)(2,1)}) %reduce-scatter.5.cloned.1.call-update) | async-done | bytes 131088 | tf_op jit(solution)/shard_map/reduce_scatter | solution.py:167
  801.0 1.6 add_convert_fusion
  (296 shorter events, 133.1 us)
Async XLA Ops:
  7.2 350.6 %all-gather.9.cloned.1.call-start = ((), (), s32[]{:S(2)}) async-start(), calls=%async_computation.3 | async-start | bytes 1179648 | tf_op jit(solution)/shard_map/all_gather | solution.py:101
  7.9 352.3 %all-gather.15.cloned.1.call-start = ((), (), s32[]{:S(2)}) async-start(), calls=%async_computation.6 | async-start | bytes 1064960 | tf_op jit(solution)/shard_map/all_gather | solution.py:110
  8.6 355.7 %all-gather.11.cloned.1.call-start = ((), (), s32[]{:S(2)}) async-start(), calls=%async_computation.4 | async-start | bytes 1064960 | tf_op jit(solution)/shard_map/all_gather | solution.py:111
  9.4 390.4 %all-gather.13.cloned.1.call-start = ((), (), s32[]{:S(2)}) async-start(), calls=%async_computation.5 | async-start | bytes 1064960 | tf_op jit(solution)/shard_map/all_gather | solution.py:109
  10.0 451.9 %all-gather.17.cloned.1.call-start = ((), (), s32[]{:S(2)}) async-start(), calls=%async_computation.7 | async-start | bytes 1064960 | tf_op jit(solution)/shard_map/all_gather | solution.py:141
  357.8 1.6 copy-start
  362.4 6.3 collective-permute-start.8
  366.1 6.3 collective-permute-start
  368.7 6.3 collective-permute-start.9
  372.4 6.3 collective-permute-start.1
  375.0 6.3 collective-permute-start.10
  376.9 127.1 %reduce-scatter.3.cloned.1.call-start = ((), (), s32[]{:S(2)}) async-start(), calls=%async_computation.8 | async-start | bytes 1179648 | tf_op jit(solution)/shard_map/reduce_scatter | solution.py:143
  378.7 6.3 collective-permute-start.2
  381.2 6.4 collective-permute-start.11
  385.0 6.5 collective-permute-start.3
  387.6 8.5 %collective-permute-start.12 = (bf16[256,2,128]{2,0,1:T(8,128)(2,1)}, bf16[256,2,128]{2,0,1:T(8,128)(2,1)}, u32[]{:S(2)}, u32[]{:S(2)}) collective-permute-start(bf16[256,2,128]{2,0,1:T(8,128)(2,1)} %collective-permute-done.11), channel_id=1, source_target_pairs={{0,8},{8,16},{16,24},{24,32},{32,40},{40,48},{48,56},{56,64},{64,7... | collective-permute-start | bytes 393224 | tf_op jit(solution)/shard_map/ppermute | solution.py:31
  391.5 10.1 %collective-permute-start.4 = (bf16[256,2,128]{0,2,1:T(8,128)(2,1)S(1)}, bf16[256,2,128]{0,2,1:T(8,128)(2,1)}, u32[]{:S(2)}, u32[]{:S(2)}) collective-permute-start(bf16[256,2,128]{0,2,1:T(8,128)(2,1)S(1)} %collective-permute-done.3), channel_id=1, source_target_pairs={{0,8},{8,16},{16,24},{24,32},{32,40},{40,48},{48,56},{56,64},{64,7... | collective-permute-start | bytes 393224 | tf_op jit(solution)/shard_map/ppermute | solution.py:31
  396.1 10.1 %collective-permute-start.13 = (bf16[256,2,128]{2,0,1:T(8,128)(2,1)}, bf16[256,2,128]{2,0,1:T(8,128)(2,1)}, u32[]{:S(2)}, u32[]{:S(2)}) collective-permute-start(bf16[256,2,128]{2,0,1:T(8,128)(2,1)} %collective-permute-done.12), channel_id=1, source_target_pairs={{0,8},{8,16},{16,24},{24,32},{32,40},{40,48},{48,56},{56,64},{64,7... | collective-permute-start | bytes 393224 | tf_op jit(solution)/shard_map/ppermute | solution.py:31
  401.6 8.6 %collective-permute-start.5 = (bf16[256,2,128]{0,2,1:T(8,128)(2,1)}, bf16[256,2,128]{0,2,1:T(8,128)(2,1)S(1)}, u32[]{:S(2)}, u32[]{:S(2)}) collective-permute-start(bf16[256,2,128]{0,2,1:T(8,128)(2,1)} %collective-permute-done.4), channel_id=1, source_target_pairs={{0,8},{8,16},{16,24},{24,32},{32,40},{40,48},{48,56},{56,64},{64,7... | collective-permute-start | bytes 393224 | tf_op jit(solution)/shard_map/ppermute | solution.py:31
  406.2 8.7 %collective-permute-start.14 = (bf16[256,2,128]{2,0,1:T(8,128)(2,1)}, bf16[256,2,128]{2,0,1:T(8,128)(2,1)S(1)}, u32[]{:S(2)}, u32[]{:S(2)}) collective-permute-start(bf16[256,2,128]{2,0,1:T(8,128)(2,1)} %collective-permute-done.13), channel_id=1, source_target_pairs={{0,8},{8,16},{16,24},{24,32},{32,40},{40,48},{48,56},{56,64},{64,7... | collective-permute-start | bytes 393224 | tf_op jit(solution)/shard_map/ppermute | solution.py:31
  410.2 8.7 %collective-permute-start.6 = (bf16[256,2,128]{0,2,1:T(8,128)(2,1)S(1)}, bf16[256,2,128]{0,2,1:T(8,128)(2,1)S(1)}, u32[]{:S(2)}, u32[]{:S(2)}) collective-permute-start(bf16[256,2,128]{0,2,1:T(8,128)(2,1)S(1)} %collective-permute-done.5), channel_id=1, source_target_pairs={{0,8},{8,16},{16,24},{24,32},{32,40},{40,48},{48,56},{56,64},{64,7... | collective-permute-start | bytes 393224 | tf_op jit(solution)/shard_map/ppermute | solution.py:31
  415.0 8.9 %collective-permute-start.15 = (bf16[256,2,128]{2,0,1:T(8,128)(2,1)S(1)}, bf16[256,2,128]{2,0,1:T(8,128)(2,1)S(1)}, u32[]{:S(2)}, u32[]{:S(2)}) collective-permute-start(bf16[256,2,128]{2,0,1:T(8,128)(2,1)S(1)} %collective-permute-done.14), channel_id=1, source_target_pairs={{0,8},{8,16},{16,24},{24,32},{32,40},{40,48},{48,56},{56,64},{64,7... | collective-permute-start | bytes 393224 | tf_op jit(solution)/shard_map/ppermute | solution.py:31
  418.9 8.1 %collective-permute-start.7 = (bf16[256,2,128]{0,2,1:T(8,128)(2,1)S(1)}, bf16[256,2,128]{0,2,1:T(8,128)(2,1)S(1)}, u32[]{:S(2)}, u32[]{:S(2)}) collective-permute-start(bf16[256,2,128]{0,2,1:T(8,128)(2,1)S(1)} %collective-permute-done.6), channel_id=1, source_target_pairs={{0,8},{8,16},{16,24},{24,32},{32,40},{40,48},{48,56},{56,64},{64,7... | collective-permute-start | bytes 393224 | tf_op jit(solution)/shard_map/ppermute | solution.py:31
  427.0 1.6 copy-start.5
  427.0 2.6 copy-start.3
  427.0 2.6 copy-start.4
  428.5 1.1 copy-start.6
  429.6 6.0 copy-start.7
  461.9 42.1 %copy-start.2 = (bf16[256,256]{1,0:T(8,128)(2,1)S(1)}, bf16[256,256]{1,0:T(8,128)(2,1)}, u32[]{:S(2)}) copy-start(bf16[256,256]{1,0:T(8,128)(2,1)} %param.12) | copy-start | bytes 393220
  464.7 124.4 %all-gather.19.cloned.1.call-start = ((), (), s32[]{:S(2)}) async-start(), calls=%async_computation.9 | async-start | bytes 2129920 | tf_op jit(solution)/shard_map/all_gather | solution.py:161
  465.5 207.6 %all-gather.21.cloned.1.call-start = ((), (), s32[]{:S(2)}) async-start(), calls=%async_computation.10 | async-start | bytes 2129920 | tf_op jit(solution)/shard_map/all_gather | solution.py:162
  466.2 290.9 %all-gather.23.cloned.1.call-start = ((), (), s32[]{:S(2)}) async-start(), calls=%async_computation.11 | async-start | bytes 2129920 | tf_op jit(solution)/shard_map/all_gather | solution.py:165
  467.0 334.0 %reduce-scatter.5.cloned.1.call-start = ((), (), s32[]{:S(2)}) async-start(), calls=%async_computation.12 | async-start | bytes 1179648 | tf_op jit(solution)/shard_map/reduce_scatter | solution.py:167
  591.4 170.3 %copy-start.8 = (s32[16]{0:T(128)S(1)}, s32[16]{0:T(128)}, u32[]{:S(2)}) copy-start(s32[16]{0:T(128)} %param.14) | copy-start | bytes 196
  763.3 39.3 %copy-start.1 = (bf16[2,16,16,256]{3,2,1,0:T(8,128)(2,1)}, bf16[2,16,16,256]{3,2,1,0:T(8,128)(2,1)S(1)}, u32[]{:S(2)}) copy-start(bf16[2,16,16,256]{3,2,1,0:T(8,128)(2,1)S(1)} %scatter_fusion) | copy-start | bytes 786436
Sparse Core Ops, SparseCore 0:
  10.0 46.6 all-gather.8
  60.1 81.1 all-gather.14
  144.6 79.8 all-gather.10
  227.7 79.7 all-gather.12
  377.0 84.8 all-gather.16
  464.8 39.1 reduce-scatter.2
  507.3 81.7 all-gather.18
  592.5 80.5 all-gather.20
  676.5 80.5 all-gather.22
  761.8 39.0 reduce-scatter.4
